TPU v7x, 32 devices: a whole 2x2x4 slice. The times are simulated.
32 devices in a mesh: scene: 2 (over y), step: 4 (over x, core), seq: 4 (over z).
Axes of the slice: x: 2, y: 2, z: 4, core: 2. Of those that a mesh axis runs over, the one named last changes fastest.
Arguments:
- queries: bfloat16 [32, 2, 24, 32, 128], P(('scene', 'step'), None, None, 'seq'), parts along dimension 0, may hold values from -256 to 256
- keys: bfloat16 [32, 2, 24, 32, 128], P(('scene', 'step'), None, None, 'seq'), parts along dimension 0, may hold values from -8 to 8
- values: bfloat16 [32, 2, 24, 32, 128], P(('scene', 'step'), None, None, 'seq'), parts along dimension 0, may hold values from -6 to 6
- start_latent: float32 [128, 32], P('scene', 'seq'), parts along dimension 0, may hold values from -6 to 6
- out_weight: bfloat16 [64, 3072], replicated, may hold values from -0.109375 to 0.109375
- cfg_table: float32 [8], replicated, may hold values from 3 to 8
- cfg_index: int32 [2], P('scene'), parts along dimension 0, may hold values from 0 to 7
- step_table: float32 [1000], replicated, may hold values from 0.03 to 0.12
- time_index: int32 [32], P(('scene', 'step')), parts along dimension 0, may hold values from 0 to 999
Outputs:
- new_iterates: float32 [32, 64, 32], P(('scene', 'step'), None, 'seq'), parts along dimension 0
There are 2 independent parts, one for each index of `scene`. A program takes and returns all parts, laid end to end along the dimension named above; an argument that names none is the same for every part. Nothing has to cross between parts.
All inputs are finite; a program needn't handle non-finite values.
Results may differ from a plain program's by a relative error of at most 0.0034.
Values may be sent and summed in bfloat16 or wider, within the bound.
No kernel may reach another device: no remote copies, remote signals or barrier semaphores. Data moves between devices by JAX's collectives and lax.ppermute only.
A program may use at most 64 MiB of HBM per device.

v0:
```python
import jax
import jax.numpy as jnp
from jax import lax
from jax.sharding import PartitionSpec as P

HD = 128
H = 24


def lookup(table, index):
    count = table.shape[0]
    hits = index[..., None] == jnp.arange(count, dtype=jnp.int32)
    return jnp.sum(jnp.where(hits, table, jnp.zeros((), table.dtype)), axis=-1)


def attend(query_rows, key_rows, value_rows):
    length = query_rows.shape[0]
    block_rows = min(512, length)
    scale = HD ** (-0.5)

    def one_block(query_block):
        scores = jnp.dot(query_block, key_rows.T, preferred_element_type=jnp.float32) * scale
        expo = jnp.exp(scores - jnp.max(scores, axis=-1, keepdims=True))
        total = jnp.sum(expo, axis=-1, keepdims=True)
        weights = expo.astype(jnp.bfloat16)
        return (jnp.dot(weights, value_rows, preferred_element_type=jnp.float32) / total).astype(
            jnp.bfloat16
        )

    blocks = query_rows.reshape(length // block_rows, block_rows, query_rows.shape[1])
    return lax.map(one_block, blocks).reshape(query_rows.shape)


def attend_items(pieces):
    query_all, key_all, value_all = pieces
    outputs = lax.map(
        lambda trio: attend(trio[0], trio[1], trio[2]), (query_all[0], key_all[0], value_all[0])
    )
    return outputs[None]


def on_device(
    queries, keys, values, start_latent, out_weight, cfg_table, cfg_index, step_table, time_index
):
    step_dev, branches, heads, tok_dev, head_size = queries.shape
    groups = lax.axis_size("seq")
    items = step_dev * branches * heads

    def to_items(array):
        return array.reshape(groups, items // groups, tok_dev, head_size)

    gathered = attend_items(
        (
            lax.all_to_all(to_items(queries), "seq", split_axis=0, concat_axis=2, tiled=True),
            lax.all_to_all(to_items(keys), "seq", split_axis=0, concat_axis=2, tiled=True),
            lax.all_to_all(to_items(values), "seq", split_axis=0, concat_axis=2, tiled=True),
        )
    )
    returned = lax.all_to_all(gathered, "seq", split_axis=2, concat_axis=0, tiled=True)
    heads_out = returned.reshape(step_dev, branches, heads, tok_dev, head_size)
    wide_out = heads_out.astype(jnp.float32)
    square_sum = jnp.sum(wide_out * wide_out, axis=(2, 4))
    root_mean = jnp.sqrt(square_sum / (H * HD) + 1e-06)
    weight_heads = out_weight.reshape(out_weight.shape[0], heads, head_size)
    drift = (
        jnp.einsum("chd,sbhld->sbcl", weight_heads, heads_out, preferred_element_type=jnp.float32)
        / root_mean[:, :, None, :]
    )
    guide_scale = lookup(cfg_table, cfg_index)[0]
    guided = drift[:, 1] + guide_scale * (drift[:, 0] - drift[:, 1])
    step_len = lookup(step_table, time_index)
    local_cum = jnp.cumsum(step_len[:, None, None] * guided, axis=0)
    group_total = local_cum[-1]
    every_total = lax.all_gather(group_total[None], "step", axis=0, tiled=True)
    position = lax.axis_index("step")
    order = jnp.arange(every_total.shape[0], dtype=jnp.int32)
    earlier = jnp.sum(
        jnp.where((order < position)[:, None, None], every_total, jnp.zeros((), jnp.float32)),
        axis=0,
    )
    return start_latent[None] + earlier[None] + local_cum


def solution(mesh):
    return jax.shard_map(
        on_device,
        mesh=mesh,
        in_specs=(
            P(("scene", "step"), None, None, "seq", None),
            P(("scene", "step"), None, None, "seq", None),
            P(("scene", "step"), None, None, "seq", None),
            P("scene", "seq"),
            P(),
            P(),
            P("scene"),
            P(),
            P(("scene", "step")),
        ),
        out_specs=P(("scene", "step"), None, "seq"),
        check_vma=False,
    )
```

profile of v0, /device:TPU:0, one launch (start us, length us, event | category | flops | bytes accessed | tf_op | source)
XLA Modules:
  0.0 86.2 jit_solution(12332049900195506394)
XLA Ops:
  0.0 18.1 %all_to_all.60 = bf16[4,48,8,128]{3,2,1,0:T(8,128)(2,1)S(1)} all-to-all(bf16[4,48,8,128]{3,2,1,0:T(8,128)(2,1)} %bitcast.96), channel_id=1, replica_groups=mesh['scene'=2,'step'=4,'seq'=4] {'seq'}, dimensions={0} | all-to-all | bytes 786432 | tf_op jit(solution)/shard_map/all_to_all | solution.py:56
  18.1 13.7 %all_to_all.61 = bf16[4,48,8,128]{3,2,1,0:T(8,128)(2,1)S(1)} all-to-all(bf16[4,48,8,128]{3,2,1,0:T(8,128)(2,1)S(1)} %bitcast.97), channel_id=1, replica_groups=mesh['scene'=2,'step'=4,'seq'=4] {'seq'}, dimensions={0} | all-to-all | bytes 786432 | tf_op jit(solution)/shard_map/all_to_all | solution.py:55
  31.9 3.5 %all-to-all-start = ((bf16[4,48,8,128]{3,2,1,0:T(8,128)(2,1)}), bf16[4,48,8,128]{3,2,1,0:T(8,128)(2,1)S(1)}, u32[]{:S(2)}, u32[]{:S(2)}) async-start(bf16[4,48,8,128]{3,2,1,0:T(8,128)(2,1)} %bitcast.4), calls=%async_computation | async-start | bytes 786432 | tf_op jit(solution)/shard_map/all_to_all | solution.py:54
  35.5 10.3 %all-to-all-done = bf16[4,48,8,128]{3,2,1,0:T(8,128)(2,1)S(1)} async-done(((bf16[4,48,8,128]{3,2,1,0:T(8,128)(2,1)}), bf16[4,48,8,128]{3,2,1,0:T(8,128)(2,1)S(1)}, u32[]{:S(2)}, u32[]{:S(2)}) %all-to-all-start) | async-done | bytes 393248 | tf_op jit(solution)/shard_map/all_to_all | solution.py:54
  45.9 18.0 %while.10 = (s32[]{:T(128)}, bf16[48,32,128]{2,1,0:T(8,128)(2,1)S(1)}, bf16[48,32,128]{2,1,0:T(8,128)(2,1)S(1)}, bf16[48,32,128]{2,1,0:T(8,128)(2,1)S(1)}, bf16[48,32,128]{2,1,0:T(8,128)(2,1)S(1)}, /*index=5*/s32[]{:T(128)}) while((s32[]{:T(128)}, bf16[48,32,128]{2,1,0:T(8,128)(2,1)S(1)}, bf16[48,32,128]{2,1,0:T(8,128)(2,1)S(1)}, ...), condition=%wide.region_4.5_spmd, body=%wide.region_1.4_spmd.sunk | while | flops 538562 | bytes 60869 | solution.py:36
  46.1 0.2 fusion.38
  46.8 0.2 fusion.38
  47.6 0.2 fusion.38
  48.3 0.2 fusion.38
  49.1 0.2 fusion.38
  49.8 0.2 fusion.38
  50.6 0.2 fusion.38
  51.3 0.2 fusion.38
  51.7 0.2 fusion.38
  52.1 0.2 fusion.38
  52.5 0.2 fusion.38
  52.8 0.2 fusion.38
  53.2 0.2 fusion.38
  54.0 0.2 fusion.38
  54.7 0.2 fusion.38
  63.9 0.9 %copy.67 = bf16[48,32,128]{2,0,1:T(8,128)(2,1)} copy(bf16[48,32,128]{2,1,0:T(8,128)(2,1)S(1)} %get-tuple-element.47) | data formatting | bytes 786432 | tf_op jit(solution)/shard_map/while | solution.py:36
  64.8 3.6 %all-to-all-start.3 = ((bf16[1,48,32,128]{3,1,0,2:T(8,128)(2,1)}), bf16[1,48,32,128]{3,1,0,2:T(8,128)(2,1)S(1)}, u32[]{:S(2)}, u32[]{:S(2)}) async-start(bf16[1,48,32,128]{3,1,0,2:T(8,128)(2,1)} %bitcast.79), calls=%async_computation.3 | async-start | bytes 786432 | tf_op jit(solution)/shard_map/all_to_all | solution.py:59
  69.2 0.6 copy-done.5
  69.9 0.7 fusion.26
  70.5 0.2 select_reduce_fusion.1
  70.7 7.6 %all-to-all-done.3 = bf16[1,48,32,128]{3,1,0,2:T(8,128)(2,1)S(1)} async-done(((bf16[1,48,32,128]{3,1,0,2:T(8,128)(2,1)}), bf16[1,48,32,128]{3,1,0,2:T(8,128)(2,1)S(1)}, u32[]{:S(2)}, u32[]{:S(2)}) %all-to-all-start.3) | async-done | bytes 393248 | tf_op jit(solution)/shard_map/all_to_all | solution.py:59
  78.4 0.3 multiply_reduce_fusion
  78.7 0.3 fusion.16
  79.0 0.7 fusion.22
  79.7 5.2 %all_gather.3 = f32[4,64,8]{1,2,0:T(8,128)S(1)} all-gather(f32[1,64,8]{1,2,0:T(8,128)S(1)} %slice.15), channel_id=1, replica_groups=mesh['scene'=2,'step'=4,'seq'=4] {'step'}, dimensions={0}, use_global_device_ids=true | all-gather | bytes 10240 | tf_op jit(solution)/shard_map/all_gather | solution.py:74
  84.9 0.6 copy-done.2
  85.5 0.6 broadcast_add_fusion
  (151 shorter events, 15.3 us)
Async XLA Ops:
  0.0 18.1 %copy-start = (bf16[4,2,24,8,128]{4,3,2,1,0:T(8,128)(2,1)S(1)}, bf16[4,2,24,8,128]{4,3,2,1,0:T(8,128)(2,1)}, u32[]{:S(2)}) copy-start(bf16[4,2,24,8,128]{4,3,2,1,0:T(8,128)(2,1)} %param.12) | copy-start | bytes 1179652
  31.9 14.0 %all-to-all-start = ((bf16[4,48,8,128]{3,2,1,0:T(8,128)(2,1)}), bf16[4,48,8,128]{3,2,1,0:T(8,128)(2,1)S(1)}, u32[]{:S(2)}, u32[]{:S(2)}) async-start(bf16[4,48,8,128]{3,2,1,0:T(8,128)(2,1)} %bitcast.4), calls=%async_computation | async-start | bytes 786432 | tf_op jit(solution)/shard_map/all_to_all | solution.py:54
  64.8 3.6 %copy-start.1 = (bf16[64,3072]{1,0:T(8,128)(2,1)S(1)}, bf16[64,3072]{1,0:T(8,128)(2,1)}, u32[]{:S(2)}) copy-start(bf16[64,3072]{1,0:T(8,128)(2,1)} %param.15) | copy-start | bytes 1179652
  64.8 13.4 %all-to-all-start.3 = ((bf16[1,48,32,128]{3,1,0,2:T(8,128)(2,1)}), bf16[1,48,32,128]{3,1,0,2:T(8,128)(2,1)S(1)}, u32[]{:S(2)}, u32[]{:S(2)}) async-start(bf16[1,48,32,128]{3,1,0,2:T(8,128)(2,1)} %bitcast.79), calls=%async_computation.3 | async-start | bytes 786432 | tf_op jit(solution)/shard_map/all_to_all | solution.py:59
  69.2 1.4 %copy-start.3 = (f32[1000]{0:T(1024)S(1)}, f32[1000]{0:T(1024)}, u32[]{:S(2)}) copy-start(f32[1000]{0:T(1024)} %param.18) | copy-start | bytes 12004
  69.2 0.7 copy-start.5
  69.8 0.7 copy-start.4
  84.9 0.7 copy-start.2
where the time goes:
time: 86.6 us; the launch traced here: 86.2 us
  blocking collectives  37 us (43%)
  waiting for transfers between devices  17.9 us (21%)
  matrix products  16.4 us (19%)
  starting transfers between devices  7.05 us (8%)
  other arithmetic  3.93 us (5%)
  local copies, waits for them, and re-layouts  2.56 us (3%)
    all_to_all x1, blocking collectives, on_device(): lax.all_to_all(to_items(values), 'seq', split_axis=0, concat_axis=2, tile...  18.1 us
    all_to_all x1, blocking collectives, on_device(): lax.all_to_all(to_items(keys), 'seq', split_axis=0, concat_axis=2, tiled=...  13.7 us
    all_to_all x1, waiting for transfers between devices, on_device(): lax.all_to_all(to_items(queries), 'seq', split_axis=0, concat_axis=2, til...  10.3 us
    dot_general x48, matrix products, one_block(): jnp.dot(weights, value_rows, preferred_element_type=jnp.float32) / total  8.69 us
    all_to_all x1, waiting for transfers between devices, on_device(): lax.all_to_all(gathered, 'seq', split_axis=2, concat_axis=0, tiled=True)  7.56 us
    dot_general x48, matrix products, one_block(): jnp.dot(query_block, key_rows.T, preferred_element_type=jnp.float32) * scale  7.47 us
    all_gather x1, blocking collectives, on_device(): every_total = lax.all_gather(group_total[None], 'step', axis=0, tiled=True)  5.17 us
    all_to_all x1, starting transfers between devices, on_device(): lax.all_to_all(gathered, 'seq', split_axis=2, concat_axis=0, tiled=True)  3.59 us
  transfers between devices with their start and end apart: 2, of which 2 were waited for; matrix products, arithmetic and copies ran while one was open for 1% of the time, Pallas kernels for 0%

commit v1 on v0

--- a/solution.py
+++ b/solution.py
@@ -71,7 +71,18 @@
     step_len = lookup(step_table, time_index)
     local_cum = jnp.cumsum(step_len[:, None, None] * guided, axis=0)
     group_total = local_cum[-1]
-    every_total = lax.all_gather(group_total[None], "step", axis=0, tiled=True)
+    ways = lax.axis_size("step")
+    up = [(d, (d + 1) % ways) for d in range(ways)]
+    down = [(d, (d - 1) % ways) for d in range(ways)]
+    earlier_2, later = ([group_total[None]], [group_total[None]])
+    for _ in range(ways // 2):
+        earlier_2.append(lax.ppermute(earlier_2[-1], "step", up))
+    for _ in range((ways - 1) // 2):
+        later.append(lax.ppermute(later[-1], "step", down))
+    line = jnp.concatenate([*earlier_2[::-1], *later[1:]], axis=0)
+    every_total = jnp.roll(
+        line, (lax.axis_index("step") - ways // 2) * group_total[None].shape[0], axis=0
+    )
     position = lax.axis_index("step")
     order = jnp.arange(every_total.shape[0], dtype=jnp.int32)
     earlier = jnp.sum(

time: 86.6 us -> 88.7 us (1.024); the launches traced: 86.2 us -> 87.1 us
  blocking collectives: 37 us -> 31.9 us
  waiting for transfers between devices: 17.9 us -> 22.9 us
  starting transfers between devices: 7.05 us -> 8.77 us
    all_gather x1 -> x0, blocking collectives: 5.17 us -> none  [on_device(): every_total = lax.all_gather(group_total[None], 'step', axis=0, tiled=True)]
    ppermute x0 -> x3, waiting for transfers between devices: none -> 4.34 us  [the longest x2 4.3 us: on_device(): earlier_2.append(lax.ppermute(earlier_2[-1], 'step', up))]
    ppermute x0 -> x3, starting transfers between devices: none -> 1.72 us  [the longest x1 1.72 us: on_device(): later.append(lax.ppermute(later[-1], 'step', down))]
  transfers between devices with their start and end apart: 2 -> 5, of which waited for: 2 -> 4; matrix products, arithmetic and copies ran while one was open for 1% -> 1% of each run, Pallas kernels for 0% -> 0%
where the time goes in v1:
time: 88.7 us; the launch traced here: 87.1 us
  blocking collectives  31.9 us (36%)
  waiting for transfers between devices  22.9 us (26%)
  matrix products  16.4 us (18%)
  starting transfers between devices  8.77 us (10%)
  other arithmetic  3.93 us (4%)
  local copies, waits for them, and re-layouts  1.92 us (2%)
    all_to_all x1, blocking collectives, on_device(): lax.all_to_all(to_items(queries), 'seq', split_axis=0, concat_axis=2, til...  18.1 us
    all_to_all x1, blocking collectives, on_device(): lax.all_to_all(to_items(keys), 'seq', split_axis=0, concat_axis=2, tiled=...  13.7 us
    all_to_all x1, waiting for transfers between devices, on_device(): lax.all_to_all(to_items(values), 'seq', split_axis=0, concat_axis=2, tile...  10.3 us
    dot_general x48, matrix products, one_block(): jnp.dot(weights, value_rows, preferred_element_type=jnp.float32) / total  8.69 us
    all_to_all x1, waiting for transfers between devices, on_device(): lax.all_to_all(gathered, 'seq', split_axis=2, concat_axis=0, tiled=True)  8.2 us
    dot_general x48, matrix products, one_block(): jnp.dot(query_block, key_rows.T, preferred_element_type=jnp.float32) * scale  7.47 us
    ppermute x2, waiting for transfers between devices, on_device(): earlier_2.append(lax.ppermute(earlier_2[-1], 'step', up))  4.3 us
    all_to_all x1, starting transfers between devices, on_device(): lax.all_to_all(gathered, 'seq', split_axis=2, concat_axis=0, tiled=True)  3.59 us
  transfers between devices with their start and end apart: 5, of which 4 were waited for; matrix products, arithmetic and copies ran while one was open for 1% of the time, Pallas kernels for 0%

profile of v1, /device:TPU:0, one launch (start us, length us, event | category | flops | bytes accessed | tf_op | source)
XLA Modules:
  0.0 87.1 jit_solution(13245768310931903662)
XLA Ops:
  0.0 18.1 %all_to_all.60 = bf16[4,48,8,128]{3,2,1,0:T(8,128)(2,1)S(1)} all-to-all(bf16[4,48,8,128]{3,2,1,0:T(8,128)(2,1)} %bitcast.96), channel_id=1, replica_groups=mesh['scene'=2,'step'=4,'seq'=4] {'seq'}, dimensions={0} | all-to-all | bytes 786432 | tf_op jit(solution)/shard_map/all_to_all | solution.py:54
  18.1 13.7 %all_to_all.61 = bf16[4,48,8,128]{3,2,1,0:T(8,128)(2,1)S(1)} all-to-all(bf16[4,48,8,128]{3,2,1,0:T(8,128)(2,1)S(1)} %bitcast.97), channel_id=1, replica_groups=mesh['scene'=2,'step'=4,'seq'=4] {'seq'}, dimensions={0} | all-to-all | bytes 786432 | tf_op jit(solution)/shard_map/all_to_all | solution.py:55
  31.9 3.5 %all-to-all-start.2 = ((bf16[4,48,8,128]{3,2,1,0:T(8,128)(2,1)}), bf16[4,48,8,128]{3,2,1,0:T(8,128)(2,1)S(1)}, u32[]{:S(2)}, u32[]{:S(2)}) async-start(bf16[4,48,8,128]{3,2,1,0:T(8,128)(2,1)} %bitcast.12), calls=%async_computation.2 | async-start | bytes 786432 | tf_op jit(solution)/shard_map/all_to_all | solution.py:56
  35.5 10.3 %all-to-all-done.2 = bf16[4,48,8,128]{3,2,1,0:T(8,128)(2,1)S(1)} async-done(((bf16[4,48,8,128]{3,2,1,0:T(8,128)(2,1)}), bf16[4,48,8,128]{3,2,1,0:T(8,128)(2,1)S(1)}, u32[]{:S(2)}, u32[]{:S(2)}) %all-to-all-start.2) | async-done | bytes 393248 | tf_op jit(solution)/shard_map/all_to_all | solution.py:56
  45.9 18.0 %while.10 = (s32[]{:T(128)}, bf16[48,32,128]{2,1,0:T(8,128)(2,1)S(1)}, bf16[48,32,128]{2,1,0:T(8,128)(2,1)S(1)}, bf16[48,32,128]{2,1,0:T(8,128)(2,1)S(1)}, bf16[48,32,128]{2,1,0:T(8,128)(2,1)S(1)}, /*index=5*/s32[]{:T(128)}) while((s32[]{:T(128)}, bf16[48,32,128]{2,1,0:T(8,128)(2,1)S(1)}, bf16[48,32,128]{2,1,0:T(8,128)(2,1)S(1)}, ...), condition=%wide.region_4.5_spmd, body=%wide.region_1.4_spmd.sunk | while | flops 538562 | bytes 60877 | solution.py:36
  46.1 0.2 fusion.38
  46.8 0.2 fusion.38
  47.6 0.2 fusion.38
  48.3 0.2 fusion.38
  49.1 0.2 fusion.38
  49.8 0.2 fusion.38
  50.6 0.2 fusion.38
  51.3 0.2 fusion.38
  51.7 0.2 fusion.38
  52.1 0.2 fusion.38
  52.5 0.2 fusion.38
  52.8 0.2 fusion.38
  53.2 0.2 fusion.38
  54.0 0.2 fusion.38
  63.9 0.9 %copy.67 = bf16[48,32,128]{2,0,1:T(8,128)(2,1)} copy(bf16[48,32,128]{2,1,0:T(8,128)(2,1)S(1)} %get-tuple-element.47) | data formatting | bytes 786432 | tf_op jit(solution)/shard_map/while | solution.py:36
  64.8 3.6 %all-to-all-start.3 = ((bf16[1,48,32,128]{3,1,0,2:T(8,128)(2,1)}), bf16[1,48,32,128]{3,1,0,2:T(8,128)(2,1)S(1)}, u32[]{:S(2)}, u32[]{:S(2)}) async-start(bf16[1,48,32,128]{3,1,0,2:T(8,128)(2,1)} %bitcast.79), calls=%async_computation.3 | async-start | bytes 786432 | tf_op jit(solution)/shard_map/all_to_all | solution.py:59
  69.2 0.7 fusion.26
  69.9 0.2 select_reduce_fusion.1
  70.1 8.2 %all-to-all-done.3 = bf16[1,48,32,128]{3,1,0,2:T(8,128)(2,1)S(1)} async-done(((bf16[1,48,32,128]{3,1,0,2:T(8,128)(2,1)}), bf16[1,48,32,128]{3,1,0,2:T(8,128)(2,1)S(1)}, u32[]{:S(2)}, u32[]{:S(2)}) %all-to-all-start.3) | async-done | bytes 393248 | tf_op jit(solution)/shard_map/all_to_all | solution.py:59
  78.4 0.3 multiply_reduce_fusion
  78.7 0.3 fusion.16
  79.0 0.7 fusion.22
  79.7 3.0 %collective-permute-done = f32[1,64,8]{1,2,0:T(8,128)S(1)} collective-permute-done((f32[1,64,8]{1,2,0:T(8,128)S(1)}, f32[1,64,8]{1,2,0:T(8,128)S(1)}, u32[]{:S(2)}, u32[]{:S(2)}) %collective-permute-start) | collective-permute-done | bytes 2080 | tf_op jit(solution)/shard_map/ppermute | solution.py:79
  82.7 1.7 %collective-permute-start.2 = (f32[1,64,8]{1,2,0:T(8,128)S(1)}, f32[1,64,8]{1,2,0:T(8,128)S(1)}, u32[]{:S(2)}, u32[]{:S(2)}) collective-permute-start(f32[1,64,8]{1,2,0:T(8,128)S(1)} %slice.15), channel_id=1, source_target_pairs={{0,12},{4,0},{8,4},{12,8},{1,13},{5,1},{9,5},{13,9},{2,14},{6,2},{... | collective-permute-start | bytes 6152 | tf_op jit(solution)/shard_map/ppermute | solution.py:81
  84.5 1.3 %collective-permute-done.1 = f32[1,64,8]{1,2,0:T(8,128)S(1)} collective-permute-done((f32[1,64,8]{1,2,0:T(8,128)S(1)}, f32[1,64,8]{1,2,0:T(8,128)S(1)}, u32[]{:S(2)}, u32[]{:S(2)}) %collective-permute-start.1) | collective-permute-done | bytes 2080 | tf_op jit(solution)/shard_map/ppermute | solution.py:79
  85.9 0.6 copy-done.2
  86.5 0.6 broadcast_add_fusion
  (164 shorter events, 15.6 us)
Async XLA Ops:
  0.0 18.1 %copy-start = (bf16[4,2,24,8,128]{4,3,2,1,0:T(8,128)(2,1)S(1)}, bf16[4,2,24,8,128]{4,3,2,1,0:T(8,128)(2,1)}, u32[]{:S(2)}) copy-start(bf16[4,2,24,8,128]{4,3,2,1,0:T(8,128)(2,1)} %param.12) | copy-start | bytes 1179652
  31.9 14.0 %all-to-all-start.2 = ((bf16[4,48,8,128]{3,2,1,0:T(8,128)(2,1)}), bf16[4,48,8,128]{3,2,1,0:T(8,128)(2,1)S(1)}, u32[]{:S(2)}, u32[]{:S(2)}) async-start(bf16[4,48,8,128]{3,2,1,0:T(8,128)(2,1)} %bitcast.12), calls=%async_computation.2 | async-start | bytes 786432 | tf_op jit(solution)/shard_map/all_to_all | solution.py:56
  64.8 3.6 %copy-start.1 = (bf16[64,3072]{1,0:T(8,128)(2,1)S(1)}, bf16[64,3072]{1,0:T(8,128)(2,1)}, u32[]{:S(2)}) copy-start(bf16[64,3072]{1,0:T(8,128)(2,1)} %param.15) | copy-start | bytes 1179652
  64.8 13.4 %all-to-all-start.3 = ((bf16[1,48,32,128]{3,1,0,2:T(8,128)(2,1)}), bf16[1,48,32,128]{3,1,0,2:T(8,128)(2,1)S(1)}, u32[]{:S(2)}, u32[]{:S(2)}) async-start(bf16[1,48,32,128]{3,1,0,2:T(8,128)(2,1)} %bitcast.79), calls=%async_computation.3 | async-start | bytes 786432 | tf_op jit(solution)/shard_map/all_to_all | solution.py:59
  68.4 0.7 copy-start.5
  68.5 1.4 %copy-start.3 = (f32[1000]{0:T(1024)S(1)}, f32[1000]{0:T(1024)}, u32[]{:S(2)}) copy-start(f32[1000]{0:T(1024)} %param.18) | copy-start | bytes 12004
  69.2 0.7 copy-start.4
  79.7 3.0 %collective-permute-start = (f32[1,64,8]{1,2,0:T(8,128)S(1)}, f32[1,64,8]{1,2,0:T(8,128)S(1)}, u32[]{:S(2)}, u32[]{:S(2)}) collective-permute-start(f32[1,64,8]{1,2,0:T(8,128)S(1)} %slice.15), channel_id=1, source_target_pairs={{0,4},{4,8},{8,12},{12,0},{1,5},{5,9},{9,13},{13,1},{2,6},{6,10},{... | collective-permute-start | bytes 6152 | tf_op jit(solution)/shard_map/ppermute | solution.py:79
  82.7 3.0 %collective-permute-start.1 = (f32[1,64,8]{1,2,0:T(8,128)S(1)}, f32[1,64,8]{1,2,0:T(8,128)S(1)}, u32[]{:S(2)}, u32[]{:S(2)}) collective-permute-start(f32[1,64,8]{1,2,0:T(8,128)S(1)} %collective-permute-done), channel_id=1, source_target_pairs={{0,4},{4,8},{8,12},{12,0},{1,5},{5,9},{9,13},{13,1},{2,6},{6,10},{... | collective-permute-start | bytes 6152 | tf_op jit(solution)/shard_map/ppermute | solution.py:79
  82.7 3.0 %collective-permute-start.2 = (f32[1,64,8]{1,2,0:T(8,128)S(1)}, f32[1,64,8]{1,2,0:T(8,128)S(1)}, u32[]{:S(2)}, u32[]{:S(2)}) collective-permute-start(f32[1,64,8]{1,2,0:T(8,128)S(1)} %slice.15), channel_id=1, source_target_pairs={{0,12},{4,0},{8,4},{12,8},{1,13},{5,1},{9,5},{13,9},{2,14},{6,2},{... | collective-permute-start | bytes 6152 | tf_op jit(solution)/shard_map/ppermute | solution.py:81
  85.8 0.7 copy-start.2
